TPU v7x, 256 devices: a whole 4x4x8 slice. The times are simulated.
256 devices in a mesh: seq: 16 (over z, core), head: 16 (over x, y).
Axes of the slice: x: 4, y: 4, z: 8, core: 2. Of those that a mesh axis runs over, the one named last changes fastest.
Arguments:
- hidden_in: bfloat16 [4, 128, 2048], P(None, None, 'seq'), may hold values from -6 to 6
- attn_gain: float32 [2048], P('seq'), may hold values from 0.1 to 1.9
- attn_router: bfloat16 [2048, 8], P('seq'), may hold values from -0.125 to 0.125
- query_weight: bfloat16 [2048, 8, 2048], P('seq', None, 'head'), may hold values from -0.125 to 0.125
- kv_weight: bfloat16 [2048, 4096], P('seq', 'head'), may hold values from -0.125 to 0.125
- out_weight: bfloat16 [8, 2048, 2048], P(None, 'head', 'seq'), may hold values from -0.09375 to 0.09375
- mlp_gain: float32 [2048], replicated, may hold values from 0.1 to 1.9
- mlp_router: bfloat16 [2048, 8], replicated, may hold values from -0.125 to 0.125
- gate_weight: bfloat16 [2048, 45056], P(None, ('seq', 'head')), may hold values from -0.125 to 0.125
- up_weight: bfloat16 [2048, 45056], P(None, ('seq', 'head')), may hold values from -0.125 to 0.125
- down_weight: bfloat16 [45056, 2048], P(('seq', 'head')), may hold values from -0.3125 to 0.3125
- cache: bfloat16 [196608, 4096], P('seq', 'head'), as said below
- token_req: int32 [196608], P('seq'), may hold values from -1 to 127, as said below
- attn_route: int32 [4, 128, 2], replicated, may hold values from 0 to 7, all different within a row
- mlp_route: int32 [4, 128, 2], replicated, may hold values from 0 to 7, all different within a row; in each aligned block of 512 rows (0 to 511, 512 to 1023, ..., all dimensions but the last counted through in order) at most 192 rows name the same one
- owner: int32 [128], replicated, may hold values from 0 to 15, as said below
Outputs:
- hidden_out: bfloat16 [4, 128, 2048], P(None, 'head', 'seq')
- new_cache: bfloat16 [160, 4, 4096], P('seq', None, 'head')
Inputs may be any that keep to these rules, and one draw needn't show every extreme that they name: `token_req`: slots form pages of 128; the live slots of a page belong to one request; request r has lengths[r] live slots; four requests have exactly 32768, every other at least one and less than 512. At most 10 requests share an owner, and some owner has exactly 10. `cache`: rows of empty slots hold values too. `attn_route`: the 2 experts of a token differ. `mlp_route`: the 2 experts of a token differ; over all 4 x 128 tokens no expert is chosen more than 192 times, and one is chosen exactly 192 times.
All inputs are finite; a program needn't handle non-finite values.
Results may differ from a plain program's by a relative error of at most 0.019.
Values may be sent and summed in bfloat16 or wider, within the bound.
No kernel may reach another device: no remote copies, remote signals or barrier semaphores. Data moves between devices by JAX's collectives and lax.ppermute only.
A program may use at most 64 MiB of HBM per device.

v0:
```python
import math
import jax
import jax.numpy as jnp
from jax import lax
from jax.sharding import PartitionSpec as P

D = 2048
HD = 128
FF = 5632
PAGE = 128
OWN_MAX = 10
epsilon = 1e-06
masked_score = -1e30


def frequency(width):
    return jnp.power(jnp.float32(10000.0), -2.0 * jnp.arange(width // 2, dtype=jnp.float32) / width)


def rotate(values, angles):
    half_width = values.shape[-1] // 2
    cosine = jnp.cos(angles)
    sine_part = jnp.sin(angles)
    lower_half = values[..., :half_width]
    upper_half = values[..., half_width:]
    return jnp.concatenate(
        [
            lower_half * cosine - upper_half * sine_part,
            upper_half * cosine + lower_half * sine_part,
        ],
        axis=-1,
    )


def on_device(
    hidden_in,
    attn_gain,
    attn_router,
    query_weight,
    kv_weight,
    out_weight,
    mlp_gain,
    mlp_router,
    gate_weight,
    up_weight,
    down_weight,
    cache,
    token_req,
    attn_route,
    mlp_route,
    owner,
):
    highest = lax.Precision.HIGHEST
    step_count, req_count, local_width = hidden_in.shape
    head_count = lax.axis_size("head")
    seq_index = lax.axis_index("seq")
    head_index = lax.axis_index("head")
    experts = query_weight.shape[1]
    heads_dev = kv_weight.shape[1] // (2 * HD)
    top_count = attn_route.shape[2]
    tok_rows = step_count * req_count
    queries_all = step_count * top_count
    hidden_f = hidden_in.astype(jnp.float32)
    squares = jnp.sum(hidden_f * hidden_f, axis=2)
    scaled = (hidden_f * attn_gain).astype(jnp.bfloat16).reshape(tok_rows, local_width)
    query_part = jnp.dot(
        scaled,
        query_weight.reshape(local_width, experts * heads_dev * HD),
        preferred_element_type=jnp.float32,
    ).reshape(step_count, req_count, experts, heads_dev * HD)
    kv_part = jnp.dot(scaled, kv_weight, preferred_element_type=jnp.float32).reshape(
        step_count, req_count, heads_dev * 2 * HD
    )
    logit_part = jnp.dot(scaled, attn_router, preferred_element_type=jnp.float32).reshape(
        step_count, req_count, experts
    )
    request_ids = jnp.arange(req_count, dtype=jnp.int32)
    counts = jnp.sum((token_req[:, None] == request_ids[None, :]).astype(jnp.float32), axis=0)
    attn_hot = (attn_route[..., None] == jnp.arange(experts, dtype=jnp.int32)).astype(jnp.float32)
    query_sum, kv_sum, logit_sum, square_sum, lengths = lax.psum(
        (query_part, kv_part, logit_part, squares, counts), "seq"
    )
    picked = jnp.einsum("srke,srec->srkc", attn_hot, query_sum, precision=highest)
    inverse = lax.rsqrt(square_sum / D + epsilon)
    attn_gates = jax.nn.softmax(
        jnp.sum(attn_hot * (logit_sum * inverse[..., None])[:, :, None, :], axis=3), axis=2
    )
    positions = lengths[None, :] + jnp.arange(step_count, dtype=jnp.float32)[:, None]
    freq_table = frequency(HD)
    queries = (picked * inverse[..., None, None]).reshape(
        step_count, req_count, top_count, heads_dev, HD
    )
    queries = rotate(queries, positions[:, :, None, None, None] * freq_table).astype(jnp.bfloat16)
    projected = kv_sum.reshape(step_count, req_count, heads_dev, 2 * HD) * inverse[..., None, None]
    new_keys = rotate(projected[..., :HD], positions[:, :, None, None] * freq_table).astype(
        jnp.bfloat16
    )
    new_values = projected[..., HD:].astype(jnp.bfloat16)
    new_rows = jnp.concatenate([new_keys, new_values], axis=3).reshape(
        step_count, req_count, heads_dev * 2 * HD
    )
    owned_flag = (owner == seq_index).astype(jnp.int32)
    before = (request_ids[None, :] < request_ids[:, None]).astype(jnp.int32)
    slot_rank = jnp.sum(before * owned_flag[None, :], axis=1)
    slot_ids = jnp.arange(OWN_MAX, dtype=jnp.int32)
    select = ((owned_flag[None, :] == 1) & (slot_rank[None, :] == slot_ids[:, None])).astype(
        jnp.bfloat16
    )
    appended = jnp.einsum(
        "jr,src->jsc", select, new_rows, preferred_element_type=jnp.float32
    ).astype(jnp.bfloat16)
    page_total = token_req.shape[0] // PAGE
    page_owner = token_req.reshape(page_total, PAGE)
    page_req = jnp.max(page_owner, axis=1)
    page_pick = jnp.maximum(page_req, 0)
    live_slot = page_owner >= 0
    req_hot = (page_req[None, :] == request_ids[:, None]).astype(jnp.float32)
    query_rows = jnp.transpose(queries, (1, 3, 0, 2, 4)).reshape(
        req_count, heads_dev, queries_all, HD
    )
    page_queries = query_rows[page_pick]
    paged = cache.reshape(page_total, PAGE, heads_dev, 2 * HD)
    score_scale = 1.0 / math.sqrt(HD)
    scores = (
        jnp.einsum(
            "phqd,pthd->phqt", page_queries, paged[..., :HD], preferred_element_type=jnp.float32
        )
        * score_scale
    )
    scores = jnp.where(live_slot[:, None, None, :], scores, masked_score)
    fresh_keys = jnp.transpose(new_keys, (1, 2, 0, 3))
    fresh_values = jnp.transpose(new_values, (1, 2, 0, 3))
    fresh_scores = (
        jnp.einsum("rhqd,rhsd->rhqs", query_rows, fresh_keys, preferred_element_type=jnp.float32)
        * score_scale
    )
    query_step = jnp.arange(queries_all) // top_count
    causal = jnp.arange(step_count)[None, :] <= query_step[:, None]
    fresh_live = causal[None, None, :, :] & (owned_flag[:, None, None, None] == 1)
    fresh_scores = jnp.where(fresh_live, fresh_scores, masked_score)
    page_best = jnp.max(scores, axis=3)
    local_best = jnp.max(
        jnp.where(req_hot[:, :, None, None] > 0, page_best[None], masked_score), axis=1
    )
    local_best = jnp.maximum(local_best, jnp.max(fresh_scores, axis=3))
    maxima = lax.pmax(local_best, "seq")
    page_probs = jnp.where(
        live_slot[:, None, None, :], jnp.exp(scores - maxima[page_pick][..., None]), 0.0
    )
    page_sums = jnp.sum(page_probs, axis=3)
    page_out = jnp.einsum(
        "phqt,pthd->phqd",
        page_probs.astype(jnp.bfloat16),
        paged[..., HD:],
        preferred_element_type=jnp.float32,
    )
    fresh_probs = jnp.where(fresh_live, jnp.exp(fresh_scores - maxima[..., None]), 0.0)
    totals = jnp.einsum("rp,phq->rhq", req_hot, page_sums, precision=highest) + jnp.sum(
        fresh_probs, axis=3
    )
    outputs = jnp.einsum("rp,phqd->rhqd", req_hot, page_out, precision=highest)
    outputs = outputs + jnp.einsum(
        "rhqs,rhsd->rhqd",
        fresh_probs.astype(jnp.bfloat16),
        fresh_values,
        preferred_element_type=jnp.float32,
    )
    local_totals = totals
    local_outputs = outputs
    totals, outputs = (
        lax.psum(local_totals.astype(jnp.bfloat16), "seq").astype(jnp.float32),
        lax.psum(local_outputs.astype(jnp.bfloat16), "seq").astype(jnp.float32),
    )
    attention = outputs / totals[..., None]
    attention = jnp.transpose(
        attention.reshape(req_count, heads_dev, step_count, top_count, HD), (2, 0, 3, 1, 4)
    )
    weighted = (attention * attn_gates[..., None, None]).astype(jnp.bfloat16)
    mixed = jnp.einsum(
        "srkhd,srke->srehd", weighted.astype(jnp.float32), attn_hot, precision=highest
    ).astype(jnp.bfloat16)
    head_part = jnp.dot(
        mixed.reshape(tok_rows, experts * heads_dev * HD),
        out_weight.reshape(experts * heads_dev * HD, local_width),
        preferred_element_type=jnp.float32,
    ).reshape(step_count, req_count, local_width)
    attn_out = lax.psum(head_part.astype(jnp.bfloat16), "head").astype(jnp.float32)
    residual = (hidden_f + attn_out).astype(jnp.bfloat16)
    full_rows = lax.all_gather(residual, "seq", axis=2, tiled=True)
    full_f = full_rows.astype(jnp.float32)
    inverse_mlp = lax.rsqrt(jnp.mean(full_f * full_f, axis=2) + epsilon)
    normed = (full_f * inverse_mlp[..., None] * mlp_gain).astype(jnp.bfloat16).reshape(tok_rows, D)
    mlp_logits = jnp.dot(normed, mlp_router, preferred_element_type=jnp.float32).reshape(
        step_count, req_count, experts
    )
    mlp_hot = (mlp_route[..., None] == jnp.arange(experts, dtype=jnp.int32)).astype(jnp.float32)
    mlp_gates = jax.nn.softmax(jnp.sum(mlp_hot * mlp_logits[:, :, None, :], axis=3), axis=2)
    combine_w = jnp.sum(mlp_hot * mlp_gates[..., None], axis=2)
    unit_count = gate_weight.shape[1]
    device_index = seq_index * head_count + head_index
    expert_index = device_index * unit_count // FF
    expert_ids = jnp.arange(experts, dtype=jnp.int32)
    rows_dev = req_count // head_count
    expert_weight = jnp.sum(
        combine_w * (expert_ids == expert_index).astype(jnp.float32), axis=2
    ).reshape(tok_rows, 1)
    gate_pre = jnp.dot(normed, gate_weight, preferred_element_type=jnp.float32)
    up_pre = jnp.dot(normed, up_weight, preferred_element_type=jnp.float32)
    hidden_units = (jax.nn.silu(gate_pre) * up_pre).astype(jnp.bfloat16)
    expert_term = (
        jnp.dot(hidden_units, down_weight, preferred_element_type=jnp.float32) * expert_weight
    ).reshape(step_count, req_count, D)
    by_columns = lax.psum_scatter(
        expert_term.astype(jnp.bfloat16), "seq", scatter_dimension=2, tiled=True
    )
    expert_part = lax.psum_scatter(by_columns, "head", scatter_dimension=1, tiled=True).astype(
        jnp.float32
    )
    own_rows = lax.dynamic_slice_in_dim(residual, head_index * rows_dev, rows_dev, 1)
    hidden_out = (own_rows.astype(jnp.float32) + expert_part).astype(jnp.bfloat16)
    return (hidden_out, appended)


def solution(mesh):
    in_specs = (
        P(None, None, "seq"),
        P("seq"),
        P("seq", None),
        P("seq", None, "head"),
        P("seq", "head"),
        P(None, "head", "seq"),
        P(),
        P(),
        P(None, ("seq", "head")),
        P(None, ("seq", "head")),
        P(("seq", "head"), None),
        P("seq", "head"),
        P("seq"),
        P(),
        P(),
        P(),
    )
    out_specs = (P(None, "head", "seq"), P("seq", None, "head"))
    return jax.shard_map(
        on_device, mesh=mesh, in_specs=in_specs, out_specs=out_specs, check_vma=False
    )
```

profile of v0, /device:TPU:2, one launch (start us, length us, event | category | flops | bytes accessed | tf_op | source)
XLA Modules:
  0.0 634.6 jit_solution(8452154288114500692)
XLA Ops:
  7.2 1.1 copy.167
  8.5 2.0 fusion.79
  10.4 2.7 fusion.67
  13.4 5.5 convert_reduce_fusion
  19.2 50.9 %all-reduce.1 = (f32[4,128]{1,0:T(4,128)S(1)}, f32[128]{0:T(128)S(1)}, f32[4,128,8]{1,2,0:T(8,128)S(1)}) all-reduce(f32[4,128]{1,0:T(4,128)S(1)} %fusion.46, f32[128]{0:T(128)S(1)} %convert_reduce_fusion, f32[4,128,8]{1,2,0:T(8,128)S(1)} %fusion.77), channel_id=1, replica_groups=mesh['seq'=16,'head'=16] {'seq'}, use_global_device_ids=true, to_apply=%region_3.0 | all-reduce | flops 4736 | bytes 37888 | tf_op jit(solution)/shard_map/psum | solution.py:80
  70.6 7.3 %select_reduce_fusion.2 = f32[4,128,2]{2,1,0:T(8,128)S(1)} fusion(f32[4,128,8]{2,1,0:T(8,128)S(1)} %copy.124, s32[4,128,2]{2,1,0:T(8,128)S(1)} %copy.111), kind=kLoop, calls=%fused_computation.46 | loop fusion | flops 23552 | bytes 24576 | tf_op jit(solution)/shard_map/reduce_sum | solution.py:86
  77.8 0.8 fusion.103
  78.8 1.0 multiply_cosine_fusion.1
  79.8 53.4 %all-reduce.14.cloned.1.call-done = (f32[4,128,256]{2,1,0:T(8,128)}, f32[4,128,8,128]{3,1,2,0:T(8,128)}) async-done(((f32[4,128,256]{2,1,0:T(8,128)}, f32[4,128,8,128]{3,1,2,0:T(8,128)}), (f32[4,128,256]{2,1,0:T(8,128)}, f32[4,128,8,128]{3,1,2,0:T(8,128)})) %all-reduce.14.cloned.1.call-update) | async-done | bytes 2621456 | tf_op jit(solution)/shard_map/psum | solution.py:80
  133.2 1.3 multiply_bitcast_fusion
  134.5 1.2 fusion.42
  135.8 3.2 fusion.12
  138.9 0.8 subtract_convert_fusion
  139.8 0.7 maximum_bitcast_fusion
  140.7 0.7 gather_fusion
  141.4 3.7 fusion.101
  145.5 0.5 fusion.102
  146.0 48.3 %pmax.7 = f32[128,1,8]{2,0,1:T(8,128)S(1)} all-reduce(f32[128,1,8]{2,0,1:T(8,128)S(1)} %maximum_bitcast_fusion.4), channel_id=1, replica_groups=mesh['seq'=16,'head'=16] {'seq'}, use_global_device_ids=true, to_apply=%region_10.0 | all-reduce | flops 1024 | bytes 8192 | tf_op jit(solution)/shard_map/pmax | solution.py:146
  194.3 0.6 gather_fusion.1
  194.9 2.9 fusion.5
  198.4 0.7 fusion.65
  199.1 1.3 fusion.21
  200.7 23.6 %psum.61 = bf16[128,8]{0,1:T(8,128)(2,1)S(1)} all-reduce(bf16[128,8]{0,1:T(8,128)(2,1)S(1)} %fusion.26), channel_id=1, replica_groups=mesh['seq'=16,'head'=16] {'seq'}, use_global_device_ids=true, to_apply=%region_14.15 | all-reduce | flops 1024 | bytes 4096 | tf_op jit(solution)/shard_map/psum | solution.py:171
  224.3 83.3 %all-reduce.8.cloned.1.call-done = bf16[128,1,8,128]{3,0,2,1:T(8,128)(2,1)} async-done(((bf16[128,1,8,128]{3,0,2,1:T(8,128)(2,1)}), bf16[128,1,8,128]{3,0,2,1:T(8,128)(2,1)}) %all-reduce.8.cloned.1.call-update) | async-done | bytes 262160 | tf_op jit(solution)/shard_map/psum | solution.py:172
  307.6 1.2 convert_divide_fusion
  308.8 2.7 convolution_convert_fusion
  311.6 1.1 fusion.25
  312.7 92.5 %all-reduce.10.cloned.1.call-done = bf16[4,128,128]{2,1,0:T(8,128)(2,1)} async-done(((bf16[4,128,128]{2,1,0:T(8,128)(2,1)}), bf16[4,128,128]{2,1,0:T(8,128)(2,1)}) %all-reduce.10.cloned.1.call-update) | async-done | bytes 131088 | tf_op jit(solution)/shard_map/psum | solution.py:187
  405.2 1.6 fusion.47
  407.1 40.6 %all-gather.2.cloned.1.call-done = bf16[4,128,2048]{2,1,0:T(8,128)(2,1)} async-done(((bf16[4,128,128]{2,1,0:T(8,128)(2,1)}), bf16[4,128,2048]{2,1,0:T(8,128)(2,1)}) %all-gather.2.cloned.1.call-update) | async-done | bytes 2097168 | tf_op jit(solution)/shard_map/all_gather | solution.py:189
  447.7 2.2 fusion.2
  450.0 0.5 fusion.4
  450.5 1.3 copy-done.2
  451.9 0.7 fusion.85
  452.6 7.3 %select_reduce_fusion.1 = f32[4,128,2]{2,1,0:T(8,128)S(1)} fusion(f32[4,128,8]{2,1,0:T(8,128)S(1)} %fusion.85, s32[4,128,2]{2,1,0:T(8,128)S(1)} %copy.126), kind=kLoop, calls=%fused_computation.44 | loop fusion | flops 23552 | bytes 24576 | tf_op jit(solution)/shard_map/reduce_sum | solution.py:197
  460.1 1.4 select_reduce_fusion
  461.7 3.5 fusion.104
  465.2 4.1 multiply_convert_fusion
  469.4 3.1 copy.133
  472.5 1.7 copy.166
  474.3 0.6 copy-done.17
  474.9 0.6 dynamic-slice
  476.2 56.6 %reduce-scatter.5.cloned.1.call-done = bf16[128,512]{1,0:T(8,128)(2,1)} async-done(((bf16[2048,512]{1,0:T(8,128)(2,1)}), bf16[128,512]{1,0:T(8,128)(2,1)}) %reduce-scatter.5.cloned.1.call-update) | async-done | bytes 131088
  532.9 0.9 reshape.447
  533.8 0.8 copy.134
  534.9 0.6 copy.129
  535.5 91.0 %all-reduce.12.cloned.1.call-done = bf16[4,128,128]{2,1,0:T(8,128)(2,1)} async-done(((bf16[4,128,128]{2,1,0:T(8,128)(2,1)}), bf16[4,128,128]{2,1,0:T(8,128)(2,1)}) %all-reduce.12.cloned.1.call-update) | async-done | bytes 131088
  626.5 1.3 add_convert_fusion.1
  (84 shorter events, 4.1 us)
Async XLA Ops:
  7.2 458.1 %copy-start = (bf16[176,2048]{1,0:T(8,128)(2,1)S(1)}, bf16[176,2048]{1,0:T(8,128)(2,1)}, u32[]{:S(2)}) copy-start(bf16[176,2048]{1,0:T(8,128)(2,1)} %param.26) | copy-start | bytes 2162692
  7.2 126.0 %all-reduce.14.cloned.1.call-start = ((), (), s32[]{:S(2)}) async-start(), calls=%async_computation.6 | async-start | bytes 5242880 | tf_op jit(solution)/shard_map/psum | solution.py:80
  10.4 2.8 copy-start.4
  10.4 3.0 copy-start.7
  10.4 8.7 %copy-start.11 = (f32[128]{0:T(128)S(1)}, f32[128]{0:T(128)}, u32[]{:S(2)}) copy-start(f32[128]{0:T(128)} %param.17) | copy-start | bytes 1540
  10.4 8.7 %copy-start.16 = (bf16[128,8]{0,1:T(8,128)(2,1)S(1)}, bf16[128,8]{0,1:T(8,128)(2,1)}, u32[]{:S(2)}) copy-start(bf16[128,8]{0,1:T(8,128)(2,1)} %param.18) | copy-start | bytes 6148
  13.1 57.1 %copy-start.12 = (s32[128]{0:T(128)S(1)}, s32[128]{0:T(128)}, u32[]{:S(2)}) copy-start(s32[128]{0:T(128)} %param.31) | copy-start | bytes 1540
  13.1 57.1 %copy-start.9 = (s32[4,128,2]{1,2,0:T(2,128)S(1)}, s32[4,128,2]{1,2,0:T(2,128)}, u32[]{:S(2)}) copy-start(s32[4,128,2]{1,2,0:T(2,128)} %param.29) | copy-start | bytes 12292
  13.2 294.5 %all-reduce.8.cloned.1.call-start = ((), (), s32[]{:S(2)}) async-start(), calls=%async_computation.1 | async-start | bytes 524288 | tf_op jit(solution)/shard_map/psum | solution.py:172
  133.2 2.6 copy-start.13
  135.7 9.7 %copy-start.5 = (bf16[4,128,1,64]{3,1,0,2:T(8,128)(2,1)}, bf16[4,128,1,64]{3,1,0,2:T(8,128)(2,1)S(1)}, u32[]{:S(2)}) copy-start(bf16[4,128,1,64]{3,1,0,2:T(8,128)(2,1)S(1)} %get-tuple-element.26) | copy-start | bytes 196612
  200.4 204.9 %all-reduce.10.cloned.1.call-start = ((), (), s32[]{:S(2)}) async-start(), calls=%async_computation.2 | async-start | bytes 262144 | tf_op jit(solution)/shard_map/psum | solution.py:187
  308.8 2.7 copy-start.14
  311.5 95.4 %copy-start.10 = (s32[4,128,2]{1,2,0:T(2,128)S(1)}, s32[4,128,2]{1,2,0:T(2,128)}, u32[]{:S(2)}) copy-start(s32[4,128,2]{1,2,0:T(2,128)} %param.30) | copy-start | bytes 12292
  311.6 138.4 %copy-start.8 = (f32[2048]{0:T(1024)S(1)}, f32[2048]{0:T(1024)}, u32[]{:S(2)}) copy-start(f32[2048]{0:T(1024)} %param.22) | copy-start | bytes 24580
  312.7 135.0 %all-gather.2.cloned.1.call-start = ((), (), s32[]{:S(2)}) async-start(), calls=%async_computation.3 | async-start | bytes 2228224 | tf_op jit(solution)/shard_map/all_gather | solution.py:189
  406.8 126.0 %reduce-scatter.5.cloned.1.call-start = ((), (), s32[]{:S(2)}) async-start(), calls=%async_computation.4 | async-start | bytes 2228224
  447.7 2.2 copy-start.1
  450.0 1.9 copy-start.15
  450.5 1.4 copy-start.2
  461.7 3.5 copy-start.3
  474.2 0.7 copy-start.17
  474.2 60.4 %copy-start.6 = (bf16[4,128,1,64]{3,1,0,2:T(8,128)(2,1)S(1)}, bf16[4,128,1,64]{3,1,0,2:T(8,128)(2,1)}, u32[]{:S(2)}) copy-start(bf16[4,128,1,64]{3,1,0,2:T(8,128)(2,1)} %copy-done.5) | copy-start | bytes 196612
  474.2 152.2 %all-reduce.12.cloned.1.call-start = ((), (), s32[]{:S(2)}) async-start(), calls=%async_computation.5 | async-start | bytes 262144
Sparse Core Ops, SparseCore 0:
  13.3 119.8 all-reduce.13
  200.5 107.0 all-reduce.7
  312.8 92.3 all-reduce.9
  407.0 40.6 all-gather.1
  474.3 58.4 reduce-scatter.4
  535.9 90.5 all-reduce.11
where the time goes:
time: 635 us
  waiting for transfers between devices  418 us (66%)
  blocking collectives  123 us (19%)
  other arithmetic  36 us (6%)
  matrix products  29.6 us (5%)
  between operations  15.3 us (2%)
  local copies, waits for them, and re-layouts  13.2 us (2%)
    unnamed x8, waiting for transfers between devices  148 us
    psum x1, waiting for transfers between devices, on_device(): lax.psum(head_part.astype(jnp.bfloat16), 'head').astype(jnp.float32)  92.5 us
    psum x1, waiting for transfers between devices, on_device(): lax.psum(local_outputs.astype(jnp.bfloat16), 'seq').astype(jnp.float32)  83.3 us
    psum x1, waiting for transfers between devices, on_device(): lax.psum((query_part, kv_part, logit_part, squares, counts), 'seq')  53.4 us
    psum x1, blocking collectives, on_device(): lax.psum((query_part, kv_part, logit_part, squares, counts), 'seq')  50.9 us
    pmax x1, blocking collectives, on_device(): maxima = lax.pmax(local_best, 'seq')  48.3 us
    all_gather x1, waiting for transfers between devices, on_device(): full_rows = lax.all_gather(residual, 'seq', axis=2, tiled=True)  40.6 us
    psum x1, blocking collectives, on_device(): lax.psum(local_totals.astype(jnp.bfloat16), 'seq').astype(jnp.float32)  23.6 us
  transfers between devices with their start and end apart: 6, of which 6 were waited for; matrix products, arithmetic and copies ran while one was open for 3% of the time, Pallas kernels for 0%

commit v1 on v0

--- a/solution.py
+++ b/solution.py
@@ -168,7 +168,9 @@
     local_totals = totals
     local_outputs = outputs
     totals, outputs = (
-        lax.psum(local_totals.astype(jnp.bfloat16), "seq").astype(jnp.float32),
+        jnp.sum(lax.all_gather(local_totals.astype(jnp.bfloat16), "seq"), axis=0).astype(
+            jnp.float32
+        ),
         lax.psum(local_outputs.astype(jnp.bfloat16), "seq").astype(jnp.float32),
     )
     attention = outputs / totals[..., None]

time: 635 us -> 635 us (level)
  blocking collectives: 123 us -> 113 us
  waiting for transfers between devices: 418 us -> 427 us
    psum x1 -> x0, blocking collectives: 23.6 us -> none  [on_device(): lax.psum(local_totals.astype(jnp.bfloat16), 'seq').astype(jnp.float32)]
    all_gather x0 -> x1, blocking collectives: none -> 14.2 us  [on_device(): lax.all_gather(local_totals.astype(jnp.bfloat16), 'seq')]
    psum x1, waiting for transfers between devices: 83.3 us -> 92.7 us  [on_device(): lax.psum(local_outputs.astype(jnp.bfloat16), 'seq').astype(jnp.float32)]
where the time goes in v1:
time: 635 us
  waiting for transfers between devices  427 us (67%)
  blocking collectives  113 us (18%)
  other arithmetic  36 us (6%)
  matrix products  29.6 us (5%)
  between operations  15.3 us (2%)
  local copies, waits for them, and re-layouts  13.2 us (2%)
    unnamed x8, waiting for transfers between devices  148 us
    psum x1, waiting for transfers between devices, on_device(): lax.psum(local_outputs.astype(jnp.bfloat16), 'seq').astype(jnp.float32)  92.7 us
    psum x1, waiting for transfers between devices, on_device(): lax.psum(head_part.astype(jnp.bfloat16), 'head').astype(jnp.float32)  92.5 us
    psum x1, waiting for transfers between devices, on_device(): lax.psum((query_part, kv_part, logit_part, squares, counts), 'seq')  53.4 us
    psum x1, blocking collectives, on_device(): lax.psum((query_part, kv_part, logit_part, squares, counts), 'seq')  50.9 us
    pmax x1, blocking collectives, on_device(): maxima = lax.pmax(local_best, 'seq')  48.3 us
    all_gather x1, waiting for transfers between devices, on_device(): full_rows = lax.all_gather(residual, 'seq', axis=2, tiled=True)  40.6 us
    all_gather x1, blocking collectives, on_device(): lax.all_gather(local_totals.astype(jnp.bfloat16), 'seq')  14.2 us
  transfers between devices with their start and end apart: 6, of which 6 were waited for; matrix products, arithmetic and copies ran while one was open for 3% of the time, Pallas kernels for 0%

profile of v1, /device:TPU:2, one launch (start us, length us, event | category | flops | bytes accessed | tf_op | source)
XLA Modules:
  0.0 634.6 jit_solution(17667059466848687357)
XLA Ops:
  7.2 1.1 copy.167
  8.5 2.0 fusion.79
  10.4 2.7 fusion.67
  13.4 5.5 convert_reduce_fusion
  19.2 50.9 %all-reduce.1 = (f32[4,128]{1,0:T(4,128)S(1)}, f32[128]{0:T(128)S(1)}, f32[4,128,8]{1,2,0:T(8,128)S(1)}) all-reduce(f32[4,128]{1,0:T(4,128)S(1)} %fusion.46, f32[128]{0:T(128)S(1)} %convert_reduce_fusion, f32[4,128,8]{1,2,0:T(8,128)S(1)} %fusion.77), channel_id=1, replica_groups=mesh['seq'=16,'head'=16] {'seq'}, use_global_device_ids=true, to_apply=%region_3.0 | all-reduce | flops 4736 | bytes 37888 | tf_op jit(solution)/shard_map/psum | solution.py:80
  70.6 7.3 %select_reduce_fusion.2 = f32[4,128,2]{2,1,0:T(8,128)S(1)} fusion(f32[4,128,8]{2,1,0:T(8,128)S(1)} %copy.124, s32[4,128,2]{2,1,0:T(8,128)S(1)} %copy.111), kind=kLoop, calls=%fused_computation.46 | loop fusion | flops 23552 | bytes 24576 | tf_op jit(solution)/shard_map/reduce_sum | solution.py:86
  77.8 0.8 fusion.103
  78.8 1.0 multiply_cosine_fusion.1
  79.8 53.4 %all-reduce.14.cloned.1.call-done = (f32[4,128,256]{2,1,0:T(8,128)}, f32[4,128,8,128]{3,1,2,0:T(8,128)}) async-done(((f32[4,128,256]{2,1,0:T(8,128)}, f32[4,128,8,128]{3,1,2,0:T(8,128)}), (f32[4,128,256]{2,1,0:T(8,128)}, f32[4,128,8,128]{3,1,2,0:T(8,128)})) %all-reduce.14.cloned.1.call-update) | async-done | bytes 2621456 | tf_op jit(solution)/shard_map/psum | solution.py:80
  133.2 1.3 multiply_bitcast_fusion
  134.5 1.2 fusion.42
  135.8 3.2 fusion.12
  138.9 0.8 subtract_convert_fusion
  139.8 0.7 maximum_bitcast_fusion
  140.7 0.7 gather_fusion
  141.4 3.7 fusion.101
  145.5 0.5 fusion.102
  146.0 48.3 %pmax.7 = f32[128,1,8]{2,0,1:T(8,128)S(1)} all-reduce(f32[128,1,8]{2,0,1:T(8,128)S(1)} %maximum_bitcast_fusion.4), channel_id=1, replica_groups=mesh['seq'=16,'head'=16] {'seq'}, use_global_device_ids=true, to_apply=%region_10.0 | all-reduce | flops 1024 | bytes 8192 | tf_op jit(solution)/shard_map/pmax | solution.py:146
  194.3 0.6 gather_fusion.1
  194.9 2.9 fusion.5
  198.4 0.7 fusion.65
  199.1 1.3 fusion.21
  200.7 14.2 %all-gather = bf16[2048,8]{0,1:T(8,128)(2,1)S(1)} all-gather(bf16[128,8]{0,1:T(8,128)(2,1)S(1)} %fusion.26), channel_id=2, replica_groups=mesh['seq'=16,'head'=16] {'seq'}, dimensions={0}, use_global_device_ids=true | all-gather | bytes 34816 | tf_op jit(solution)/shard_map/all_gather | solution.py:171
  215.0 92.7 %all-reduce.8.cloned.1.call-done = bf16[128,1,8,128]{3,0,2,1:T(8,128)(2,1)} async-done(((bf16[128,1,8,128]{3,0,2,1:T(8,128)(2,1)}), bf16[128,1,8,128]{3,0,2,1:T(8,128)(2,1)}) %all-reduce.8.cloned.1.call-update) | async-done | bytes 262160 | tf_op jit(solution)/shard_map/psum | solution.py:174
  307.6 1.2 convert_divide_fusion
  308.8 2.7 convolution_convert_fusion
  311.6 1.1 fusion.25
  312.7 92.5 %all-reduce.10.cloned.1.call-done = bf16[4,128,128]{2,1,0:T(8,128)(2,1)} async-done(((bf16[4,128,128]{2,1,0:T(8,128)(2,1)}), bf16[4,128,128]{2,1,0:T(8,128)(2,1)}) %all-reduce.10.cloned.1.call-update) | async-done | bytes 131088 | tf_op jit(solution)/shard_map/psum | solution.py:189
  405.2 1.6 fusion.47
  407.1 40.6 %all-gather.3.cloned.1.call-done = bf16[4,128,2048]{2,1,0:T(8,128)(2,1)} async-done(((bf16[4,128,128]{2,1,0:T(8,128)(2,1)}), bf16[4,128,2048]{2,1,0:T(8,128)(2,1)}) %all-gather.3.cloned.1.call-update) | async-done | bytes 2097168 | tf_op jit(solution)/shard_map/all_gather | solution.py:191
  447.7 2.2 fusion.2
  450.0 0.5 fusion.4
  450.5 1.3 copy-done.2
  451.9 0.7 fusion.85
  452.6 7.3 %select_reduce_fusion.1 = f32[4,128,2]{2,1,0:T(8,128)S(1)} fusion(f32[4,128,8]{2,1,0:T(8,128)S(1)} %fusion.85, s32[4,128,2]{2,1,0:T(8,128)S(1)} %copy.126), kind=kLoop, calls=%fused_computation.44 | loop fusion | flops 23552 | bytes 24576 | tf_op jit(solution)/shard_map/reduce_sum | solution.py:199
  460.1 1.4 select_reduce_fusion
  461.7 3.5 fusion.104
  465.2 4.1 multiply_convert_fusion
  469.4 3.1 copy.133
  472.5 1.7 copy.166
  474.3 0.6 copy-done.17
  474.9 0.6 dynamic-slice
  476.2 56.6 %reduce-scatter.5.cloned.1.call-done = bf16[128,512]{1,0:T(8,128)(2,1)} async-done(((bf16[2048,512]{1,0:T(8,128)(2,1)}), bf16[128,512]{1,0:T(8,128)(2,1)}) %reduce-scatter.5.cloned.1.call-update) | async-done | bytes 131088
  532.9 0.9 reshape.454
  533.8 0.8 copy.134
  534.9 0.6 copy.129
  535.5 91.0 %all-reduce.12.cloned.1.call-done = bf16[4,128,128]{2,1,0:T(8,128)(2,1)} async-done(((bf16[4,128,128]{2,1,0:T(8,128)(2,1)}), bf16[4,128,128]{2,1,0:T(8,128)(2,1)}) %all-reduce.12.cloned.1.call-update) | async-done | bytes 131088
  626.5 1.3 add_convert_fusion.1
  (85 shorter events, 4.1 us)
Async XLA Ops:
  7.2 458.1 %copy-start = (bf16[176,2048]{1,0:T(8,128)(2,1)S(1)}, bf16[176,2048]{1,0:T(8,128)(2,1)}, u32[]{:S(2)}) copy-start(bf16[176,2048]{1,0:T(8,128)(2,1)} %param.26) | copy-start | bytes 2162692
  7.2 126.0 %all-reduce.14.cloned.1.call-start = ((), (), s32[]{:S(2)}) async-start(), calls=%async_computation.6 | async-start | bytes 5242880 | tf_op jit(solution)/shard_map/psum | solution.py:80
  10.4 2.8 copy-start.4
  10.4 3.0 copy-start.7
  10.4 8.7 %copy-start.11 = (f32[128]{0:T(128)S(1)}, f32[128]{0:T(128)}, u32[]{:S(2)}) copy-start(f32[128]{0:T(128)} %param.17) | copy-start | bytes 1540
  10.4 8.7 %copy-start.16 = (bf16[128,8]{0,1:T(8,128)(2,1)S(1)}, bf16[128,8]{0,1:T(8,128)(2,1)}, u32[]{:S(2)}) copy-start(bf16[128,8]{0,1:T(8,128)(2,1)} %param.18) | copy-start | bytes 6148
  13.1 57.1 %copy-start.12 = (s32[128]{0:T(128)S(1)}, s32[128]{0:T(128)}, u32[]{:S(2)}) copy-start(s32[128]{0:T(128)} %param.31) | copy-start | bytes 1540
  13.1 57.1 %copy-start.9 = (s32[4,128,2]{1,2,0:T(2,128)S(1)}, s32[4,128,2]{1,2,0:T(2,128)}, u32[]{:S(2)}) copy-start(s32[4,128,2]{1,2,0:T(2,128)} %param.29) | copy-start | bytes 12292
  13.2 294.5 %all-reduce.8.cloned.1.call-start = ((), (), s32[]{:S(2)}) async-start(), calls=%async_computation.1 | async-start | bytes 524288 | tf_op jit(solution)/shard_map/psum | solution.py:174
  133.2 2.6 copy-start.13
  135.7 9.7 %copy-start.5 = (bf16[4,128,1,64]{3,1,0,2:T(8,128)(2,1)}, bf16[4,128,1,64]{3,1,0,2:T(8,128)(2,1)S(1)}, u32[]{:S(2)}) copy-start(bf16[4,128,1,64]{3,1,0,2:T(8,128)(2,1)S(1)} %get-tuple-element.26) | copy-start | bytes 196612
  200.4 204.9 %all-reduce.10.cloned.1.call-start = ((), (), s32[]{:S(2)}) async-start(), calls=%async_computation.2 | async-start | bytes 262144 | tf_op jit(solution)/shard_map/psum | solution.py:189
  308.8 2.7 copy-start.14
  311.5 95.4 %copy-start.10 = (s32[4,128,2]{1,2,0:T(2,128)S(1)}, s32[4,128,2]{1,2,0:T(2,128)}, u32[]{:S(2)}) copy-start(s32[4,128,2]{1,2,0:T(2,128)} %param.30) | copy-start | bytes 12292
  311.6 138.4 %copy-start.8 = (f32[2048]{0:T(1024)S(1)}, f32[2048]{0:T(1024)}, u32[]{:S(2)}) copy-start(f32[2048]{0:T(1024)} %param.22) | copy-start | bytes 24580
  312.7 135.0 %all-gather.3.cloned.1.call-start = ((), (), s32[]{:S(2)}) async-start(), calls=%async_computation.3 | async-start | bytes 2228224 | tf_op jit(solution)/shard_map/all_gather | solution.py:191
  406.8 126.0 %reduce-scatter.5.cloned.1.call-start = ((), (), s32[]{:S(2)}) async-start(), calls=%async_computation.4 | async-start | bytes 2228224
  447.7 2.2 copy-start.1
  450.0 1.9 copy-start.15
  450.5 1.4 copy-start.2
  461.7 3.5 copy-start.3
  474.2 0.7 copy-start.17
  474.2 60.4 %copy-start.6 = (bf16[4,128,1,64]{3,1,0,2:T(8,128)(2,1)S(1)}, bf16[4,128,1,64]{3,1,0,2:T(8,128)(2,1)}, u32[]{:S(2)}) copy-start(bf16[4,128,1,64]{3,1,0,2:T(8,128)(2,1)} %copy-done.5) | copy-start | bytes 196612
  474.2 152.2 %all-reduce.12.cloned.1.call-start = ((), (), s32[]{:S(2)}) async-start(), calls=%async_computation.5 | async-start | bytes 262144
Sparse Core Ops, SparseCore 0:
  13.3 119.8 all-reduce.13
  200.5 107.0 all-reduce.7
  312.8 92.3 all-reduce.9
  407.0 40.6 all-gather.2
  474.3 58.4 reduce-scatter.4
  535.9 90.5 all-reduce.11
